TPU v7x, 256 devices: a whole 4x4x8 slice. The times are simulated.
256 devices in a mesh: req: 32 (over y, z), head: 8 (over x, core).
Axes of the slice: x: 4, y: 4, z: 8, core: 2. Of those that a mesh axis runs over, the one named last changes fastest.
Arguments:
- tokens: bfloat16 [32768, 1024], P(('req', 'head')), may hold values from -6 to 6
- w_proj: bfloat16 [1024, 2048], P(None, 'head'), may hold values from -0.1875 to 0.1875
- w_out: bfloat16 [1024, 1024], replicated, may hold values from -0.1875 to 0.1875
- kv_cache: bfloat16 [32, 32, 3, 128, 2048], P('req', None, None, None, 'head'), may hold values from -6 to 6
- slot_request: int32 [64], P('req'), may hold values from 0 to 63, each once
- lengths: int32 [64], replicated, may hold values from 1 to 4096
- block_owner: int32 [2048, 1], P('req'), may hold values from 0 to 31; in each aligned block of 64 rows (0 to 63, 64 to 127, ...) at most 3 rows name the same one
Outputs:
- mixed: bfloat16 [32768, 1024], P(('req', 'head'))
Inputs may be any that keep to these rules, and one draw needn't show every extreme that they name: `block_owner`: within each aligned block of 64 rows no owner appears more than 3 times.
All inputs are finite; a program needn't handle non-finite values.
Results may differ from a plain program's by a relative error of at most 0.0088.
Values may be sent and summed in bfloat16 or wider, within the bound.
No kernel may reach another device: no remote copies, remote signals or barrier semaphores. Data moves between devices by JAX's collectives and lax.ppermute only.
A program may use at most 128 MiB of HBM per device.

v0:
```python
import jax
import jax.numpy as jnp
from jax import lax
from jax.sharding import PartitionSpec as P

DH = 64
CAND = 512
BLK = 128
MAXB = 32


def layer_norm(values):
    mean = jnp.mean(values, axis=-1, keepdims=True)
    square = jnp.mean(values * values, axis=-1, keepdims=True)
    return (values - mean) * lax.rsqrt(square - mean * mean + 1e-05)


def shards(tokens, w_proj, w_out, kv_cache, slot_request, lengths, block_owner):
    head_local = w_proj.shape[1] // (2 * DH)
    gathered = lax.all_gather(tokens, "head", axis=0, tiled=True)
    normed = layer_norm(gathered.astype(jnp.float32)).astype(jnp.bfloat16)
    row_count = normed.shape[0]
    slots = row_count // CAND
    proj = jax.nn.silu(jnp.dot(normed, w_proj, preferred_element_type=jnp.float32))
    proj = proj.reshape(row_count, head_local, 2, DH)
    gate_u = proj[:, :, 0].astype(jnp.bfloat16).reshape(row_count, head_local * DH)
    query = proj[:, :, 1].astype(jnp.bfloat16).reshape(slots, CAND, head_local, DH)
    received = lax.all_to_all(kv_cache, "req", split_axis=1, concat_axis=0, tiled=True)
    most_slots = received.shape[2]
    pool = received.reshape(-1, BLK, received.shape[-1])
    owner_count = lax.axis_size("req")
    owners = block_owner[:, 0]
    onehot = (owners[:, None] == jnp.arange(owner_count, dtype=jnp.int32)[None, :]).astype(
        jnp.int32
    )
    rank = jnp.sum((jnp.cumsum(onehot, axis=0) - onehot) * onehot, axis=1)
    history = pool[owners * most_slots + rank].reshape(slots, MAXB * BLK, head_local, 2, DH)
    total_requests = lengths.shape[0]
    match = slot_request[:, None] == jnp.arange(total_requests, dtype=jnp.int32)[None, :]
    slot_lengths = jnp.sum(jnp.where(match, lengths[None, :], 0), axis=1)
    positions = jnp.arange(MAXB * BLK, dtype=jnp.int32)
    scale = 1.0 / DH**0.5
    results = []
    for slot in range(slots):
        keys = history[slot, :, :, 0]
        values = history[slot, :, :, 1]
        scores = (
            jnp.einsum("chd,phd->hcp", query[slot], keys, preferred_element_type=jnp.float32)
            * scale
        )
        live = positions < slot_lengths[slot]
        weights = jnp.where(live[None, None, :], jax.nn.silu(scores), 0.0).astype(jnp.bfloat16)
        results.append(
            jnp.einsum("hcp,phd->chd", weights, values, preferred_element_type=jnp.float32)
        )
    attn = jnp.stack(results).reshape(row_count, head_local * DH).astype(jnp.bfloat16)
    width_all = w_out.shape[0]
    attn_wide = attn.astype(jnp.float32)
    first_sum, second_sum = lax.psum(
        (jnp.sum(attn_wide, axis=1), jnp.sum(attn_wide * attn_wide, axis=1)), "head"
    )
    mean = (first_sum / width_all)[:, None]
    square = (second_sum / width_all)[:, None]
    hidden = (
        (attn_wide - mean) * lax.rsqrt(square - mean * mean + 1e-05) * gate_u.astype(jnp.float32)
    )
    hidden = hidden.astype(jnp.bfloat16)
    local_width = head_local * DH
    w_rows = lax.dynamic_slice_in_dim(w_out, lax.axis_index("head") * local_width, local_width, 0)
    summed = lax.psum_scatter(
        jnp.dot(hidden, w_rows, preferred_element_type=jnp.float32),
        "head",
        scatter_dimension=0,
        tiled=True,
    )
    return summed.astype(jnp.bfloat16)


def solution(mesh):
    return jax.shard_map(
        shards,
        mesh=mesh,
        in_specs=(
            P(("req", "head"), None),
            P(None, "head"),
            P(),
            P("req", None, None, None, "head"),
            P("req"),
            P(),
            P("req", None),
        ),
        out_specs=P(("req", "head"), None),
        check_vma=False,
    )
```

profile of v0, /device:TPU:8, one launch (start us, length us, event | category | flops | bytes accessed | tf_op | source)
XLA Modules:
  0.0 321.6 jit_solution(10746997793371658407)
XLA Ops:
  6.5 0.0 copy-start
  6.5 0.0 copy-start.2
  6.5 0.0 copy-start.4
  6.5 0.0 copy-start.5
  6.5 0.0 copy-start.3
  6.5 12.0 %all-to-all-start = ((bf16[1,32,3,128,256]{4,3,2,0,1:T(8,128)(2,1)}), bf16[1,32,3,128,256]{4,3,2,0,1:T(8,128)(2,1)}, u32[]{:S(2)}, u32[]{:S(2)}) async-start(bf16[1,32,3,128,256]{4,3,2,0,1:T(8,128)(2,1)} %bitcast.58), calls=%async_computation | async-start | bytes 12582912 | tf_op jit(solution)/shard_map/all_to_all | solution.py:28
  18.6 0.0 all-gather.2.cloned.1.call-start
  18.6 0.7 all-gather.2.cloned.1.call-update
  19.3 0.0 reduce-scatter.2.cloned.1.call-start
  19.4 0.0 copy-done.2
  19.4 0.1 fusion.26
  19.5 0.1 reduce_window_sum.11
  19.6 0.2 select_reduce_fusion
  19.8 0.0 copy-done.4
  19.8 0.0 copy-done.5
  19.8 0.2 fusion.27
  20.0 0.6 fusion.38
  20.5 0.7 iota_compare_fusion.2
  21.2 0.6 iota_compare_fusion.1
  21.8 28.2 %all-gather.2.cloned.1.call-done = bf16[1024,1024]{1,0:T(8,128)(2,1)} async-done(((bf16[128,1024]{1,0:T(8,128)(2,1)}), bf16[1024,1024]{1,0:T(8,128)(2,1)}) %all-gather.2.cloned.1.call-update) | async-done | bytes 2097168 | tf_op jit(solution)/shard_map/all_gather | solution.py:20
  50.0 2.3 convert_reduce_fusion
  52.2 0.0 copy-done.3
  52.2 2.8 multiply_convert_fusion
  55.1 0.0 copy-start.1
  55.1 0.8 copy-done.1
  55.9 100.5 %all-to-all-done = bf16[1,32,3,128,256]{4,3,2,0,1:T(8,128)(2,1)} async-done(((bf16[1,32,3,128,256]{4,3,2,0,1:T(8,128)(2,1)}), bf16[1,32,3,128,256]{4,3,2,0,1:T(8,128)(2,1)}, u32[]{:S(2)}, u32[]{:S(2)}) %all-to-all-start) | async-done | bytes 6291488 | tf_op jit(solution)/shard_map/all_to_all | solution.py:28
  156.4 5.6 %gather_fusion = bf16[64,128,256]{2,1,0:T(8,128)(2,1)} fusion(bf16[96,128,256]{2,1,0:T(8,128)(2,1)} %bitcast.1, s32[1024]{0:T(1024)S(1)} %pad_clamp_fusion), kind=kCustom, calls=%fused_computation | custom fusion | bytes 8388864 | tf_op jit(solution)/shard_map/gather | solution.py:37
  162.0 15.1 %reshape.81 = bf16[2,4096,2,2,64]{4,3,2,1,0:T(2,128)(2,1)} reshape(bf16[64,128,256]{2,1,0:T(8,128)(2,1)} %gather_fusion) | data formatting | bytes 8388608 | tf_op jit(solution)/shard_map/reshape | solution.py:37
  177.1 19.4 %fusion.37 = (bf16[1,4096,2,1,64]{4,3,2,1,0:T(2,128)(2,1)}, bf16[1,4096,2,1,64]{4,3,2,1,0:T(2,128)(2,1)}, bf16[1,4096,2,1,64]{4,3,2,1,0:T(2,128)(2,1)}, bf16[1,4096,2,1,64]{4,3,2,1,0:T(2,128)(2,1)}) fusion(bf16[2,4096,2,2,64]{4,3,2,1,0:T(2,128)(2,1)} %reshape.81), kind=kLoop, calls=%fused_computation.55 | loop fusion | bytes 8388608 | tf_op jit(solution)/shard_map/slice | solution.py:46
  196.5 9.4 %copy.45 = bf16[1,4096,2,1,64]{1,4,2,3,0:T(8,128)(2,1)} copy(bf16[1,4096,2,1,64]{4,3,2,1,0:T(2,128)(2,1)} %get-tuple-element.11) | data formatting | bytes 2097152
  205.9 9.5 %copy.47 = bf16[1,4096,2,1,64]{1,4,2,3,0:T(8,128)(2,1)} copy(bf16[1,4096,2,1,64]{4,3,2,1,0:T(2,128)(2,1)} %get-tuple-element.13) | data formatting | bytes 2097152
  215.3 8.4 %copy.48 = bf16[1,4096,2,1,64]{1,4,2,3,0:T(8,128)(2,1)S(1)} copy(bf16[1,4096,2,1,64]{4,3,2,1,0:T(2,128)(2,1)} %get-tuple-element.12) | data formatting | bytes 2097152
  223.7 9.4 %copy.50 = bf16[1,4096,2,1,64]{1,4,2,3,0:T(8,128)(2,1)} copy(bf16[1,4096,2,1,64]{4,3,2,1,0:T(2,128)(2,1)} %get-tuple-element.14) | data formatting | bytes 2097152
  233.2 9.0 %fusion.10 = bf16[1,512,2,64]{1,3,2,0:T(8,128)(2,1)S(1)} fusion(pred[4096]{0:T(1024)(128)(4,1)S(1)} %iota_compare_fusion.2, bf16[1,4096,2,1,64]{1,4,2,3,0:T(8,128)(2,1)} %copy.47, bf16[1,4096,2,1,64]{1,4,2,3,0:T(8,128)(2,1)} %copy.45, bf16[1024,2,2,64]{0,3,2,1:T(8,128)(2,1)} %bitcast.63), kind=kOutput, calls=%fused_computation.15 | convolution fusion | flops 1103101952 | bytes 2363392 | tf_op jit(solution)/shard_map/hcp,phd->chd/dot_general | solution.py:54
  242.1 9.3 %fusion.9 = bf16[1,512,2,64]{1,3,2,0:T(8,128)(2,1)} fusion(pred[4096]{0:T(1024)(128)(4,1)S(1)} %iota_compare_fusion.1, bf16[1,4096,2,1,64]{1,4,2,3,0:T(8,128)(2,1)} %copy.50, bf16[1,4096,2,1,64]{1,4,2,3,0:T(8,128)(2,1)S(1)} %copy.48, bf16[1024,2,2,64]{0,3,2,1:T(8,128)(2,1)} %bitcast.64), kind=kOutput, calls=%fused_computation.14 | convolution fusion | flops 1103101952 | bytes 2363392 | tf_op jit(solution)/shard_map/hcp,phd->chd/dot_general | solution.py:54
  251.5 1.0 fusion.36
  252.5 0.9 fusion.22
  253.4 0.4 copy.42
  253.8 0.1 copy.51
  253.9 12.7 %all-reduce = (f32[1024]{0:T(1024)S(1)}, f32[1024]{0:T(1024)S(1)}) all-reduce(f32[1024]{0:T(1024)S(1)} %bitcast.68, f32[1024]{0:T(1024)S(1)} %bitcast.67), channel_id=1, replica_groups=mesh['req'=32,'head'=8] {'head'}, use_global_device_ids=true, to_apply=%region_8.9 | all-reduce | flops 2048 | bytes 16384 | tf_op jit(solution)/shard_map/psum | solution.py:59
  266.6 0.0 copy-done
  266.7 2.7 fusion.20
  269.3 0.0 reduce-scatter.2.cloned.1.call-update
  269.4 43.7 %reduce-scatter.2.cloned.1.call-done = f32[128,1024]{1,0:T(8,128)} async-done(((f32[1024,1024]{1,0:T(8,128)}), f32[128,1024]{1,0:T(8,128)}) %reduce-scatter.2.cloned.1.call-update) | async-done | bytes 524304 | tf_op jit(solution)/shard_map/reduce_scatter | solution.py:70
  313.0 1.8 convert_element_type.60
  (7 shorter events, 0.1 us)
Async XLA Ops:
  6.5 260.1 %copy-start = (bf16[1024,1024]{1,0:T(8,128)(2,1)S(1)}, bf16[1024,1024]{1,0:T(8,128)(2,1)}, u32[]{:S(2)}) copy-start(bf16[1024,1024]{1,0:T(8,128)(2,1)} %param.9) | copy-start | bytes 6291460
  6.5 12.8 %copy-start.2 = (s32[64,1]{0,1:T(1,128)S(1)}, s32[64,1]{0,1:T(1,128)}, u32[]{:S(2)}) copy-start(s32[64,1]{0,1:T(1,128)} %param.13) | copy-start | bytes 772
  6.5 13.2 %copy-start.4 = (s32[64]{0:T(128)S(1)}, s32[64]{0:T(128)}, u32[]{:S(2)}) copy-start(s32[64]{0:T(128)} %param.12) | copy-start | bytes 772
  6.5 13.2 %copy-start.5 = (s32[2]{0:T(128)S(1)}, s32[2]{0:T(128)}, u32[]{:S(2)}) copy-start(s32[2]{0:T(128)} %param.11) | copy-start | bytes 28
  6.5 45.7 %copy-start.3 = (bf16[1024,256]{1,0:T(8,128)(2,1)S(1)}, bf16[1024,256]{1,0:T(8,128)(2,1)}, u32[]{:S(2)}) copy-start(bf16[1024,256]{1,0:T(8,128)(2,1)} %param.8) | copy-start | bytes 1572868
  6.5 149.9 %all-to-all-start = ((bf16[1,32,3,128,256]{4,3,2,0,1:T(8,128)(2,1)}), bf16[1,32,3,128,256]{4,3,2,0,1:T(8,128)(2,1)}, u32[]{:S(2)}, u32[]{:S(2)}) async-start(bf16[1,32,3,128,256]{4,3,2,0,1:T(8,128)(2,1)} %bitcast.58), calls=%async_computation | async-start | bytes 12582912 | tf_op jit(solution)/shard_map/all_to_all | solution.py:28
  18.6 31.4 %all-gather.2.cloned.1.call-start = ((), (), s32[]{:S(2)}) async-start(), calls=%async_computation.2 | async-start | bytes 2359296 | tf_op jit(solution)/shard_map/all_gather | solution.py:20
  19.3 293.7 %reduce-scatter.2.cloned.1.call-start = ((), (), s32[]{:S(2)}) async-start(), calls=%async_computation.3 | async-start | bytes 4718592 | tf_op jit(solution)/shard_map/reduce_scatter | solution.py:70
  55.1 0.8 copy-start.1
Sparse Core Ops, SparseCore 0:
  21.3 28.6 all-gather.1
  269.5 43.5 reduce-scatter.1
where the time goes:
time: 323 us; the launch traced here: 322 us
  waiting for transfers between devices  173 us (54%)
  local copies, waits for them, and re-layouts  78.7 us (24%)
  matrix products  23.8 us (7%)
  between operations  13.6 us (4%)
  blocking collectives  12.7 us (4%)
  starting transfers between devices  12.1 us (4%)
  other arithmetic  7.75 us (2%)
    all_to_all x1, waiting for transfers between devices, shards(): lax.all_to_all(kv_cache, 'req', split_axis=1, concat_axis=0, tiled=True)  101 us
    reduce_scatter x1, waiting for transfers between devices, shards(): lax.psum_scatter(jnp.dot(hidden, w_rows, preferred_element_type=jnp.float...  43.7 us
    unnamed x19, local copies, waits for them, and re-layouts  37.6 us
    all_gather x1, waiting for transfers between devices, shards(): gathered = lax.all_gather(tokens, 'head', axis=0, tiled=True)  28.2 us
    slice x1, local copies, waits for them, and re-layouts, shards(): values = history[slot, :, :, 1]  19.4 us
    dot_general x2, matrix products, shards(): jnp.einsum('hcp,phd->chd', weights, values, preferred_element_type=jnp.fl...  18.3 us
    reshape x1, local copies, waits for them, and re-layouts, shards(): pool[owners * most_slots + rank]  15.1 us
    psum x1, blocking collectives, shards(): lax.psum((jnp.sum(attn_wide, axis=1), jnp.sum(attn_wide * attn_wide, axis...  12.7 us
  transfers between devices with their start and end apart: 3, of which 3 were waited for; matrix products, arithmetic and copies ran while one was open for 2% of the time, Pallas kernels for 0%

commit v1 on v0

--- a/solution.py
+++ b/solution.py
@@ -17,7 +17,9 @@
 
 def shards(tokens, w_proj, w_out, kv_cache, slot_request, lengths, block_owner):
     head_local = w_proj.shape[1] // (2 * DH)
-    gathered = lax.all_gather(tokens, "head", axis=0, tiled=True)
+    gathered = jnp.concatenate(
+        lax.all_to_all(jnp.stack([tokens] * lax.axis_size("head")), "head", 0, 0), axis=0
+    )
     normed = layer_norm(gathered.astype(jnp.float32)).astype(jnp.bfloat16)
     row_count = normed.shape[0]
     slots = row_count // CAND

time: 323 us -> 353 us (1.093)
  blocking collectives: 12.7 us -> 44.4 us
    all_to_all x0 -> x1, blocking collectives: none -> 31.7 us  [shards(): lax.all_to_all(jnp.stack([tokens] * lax.axis_size('head')), 'head', 0, 0)]
    all_gather x1 -> x0, waiting for transfers between devices: 28.2 us -> none  [shards(): gathered = lax.all_gather(tokens, 'head', axis=0, tiled=True)]
    all_to_all x1, waiting for transfers between devices: 101 us -> 127 us  [shards(): lax.all_to_all(kv_cache, 'req', split_axis=1, concat_axis=0, tiled=True)]
  transfers between devices with their start and end apart: 3 -> 2, of which waited for: 3 -> 2; matrix products, arithmetic and copies ran while one was open for 2% -> 2% of each run, Pallas kernels for 0% -> 0%
where the time goes in v1:
time: 353 us; the launch traced here: 351 us
  waiting for transfers between devices  170 us (48%)
  local copies, waits for them, and re-layouts  80 us (23%)
  blocking collectives  44.4 us (13%)
  matrix products  21.9 us (6%)
  between operations  13.6 us (4%)
  starting transfers between devices  11.9 us (3%)
  other arithmetic  9.89 us (3%)
    all_to_all x1, waiting for transfers between devices, shards(): lax.all_to_all(kv_cache, 'req', split_axis=1, concat_axis=0, tiled=True)  127 us
    reduce_scatter x1, waiting for transfers between devices, shards(): lax.psum_scatter(jnp.dot(hidden, w_rows, preferred_element_type=jnp.float...  42.4 us
    unnamed x19, local copies, waits for them, and re-layouts  37.6 us
    all_to_all x1, blocking collectives, shards(): lax.all_to_all(jnp.stack([tokens] * lax.axis_size('head')), 'head', 0, 0)  31.7 us
    slice x1, local copies, waits for them, and re-layouts, shards(): values = history[slot, :, :, 1]  19.4 us
    dot_general x2, matrix products, shards(): jnp.einsum('hcp,phd->chd', weights, values, preferred_element_type=jnp.fl...  18.3 us
    reshape x1, local copies, waits for them, and re-layouts, shards(): pool[owners * most_slots + rank]  15.1 us
    psum x1, blocking collectives, shards(): lax.psum((jnp.sum(attn_wide, axis=1), jnp.sum(attn_wide * attn_wide, axis...  12.7 us
  transfers between devices with their start and end apart: 2, of which 2 were waited for; matrix products, arithmetic and copies ran while one was open for 2% of the time, Pallas kernels for 0%

profile of v1, /device:TPU:8, one launch (start us, length us, event | category | flops | bytes accessed | tf_op | source)
XLA Modules:
  0.0 351.4 jit_solution(5504634274482203315)
XLA Ops:
  6.5 0.0 copy-start
  6.5 1.4 stack.8
  7.9 31.7 %all_to_all.14 = bf16[8,128,1024]{2,1,0:T(8,128)(2,1)} all-to-all(bf16[8,128,1024]{2,1,0:T(8,128)(2,1)S(1)} %stack.8), channel_id=1, replica_groups=mesh['req'=32,'head'=8] {'head'}, dimensions={0} | all-to-all | bytes 4194304 | tf_op jit(solution)/shard_map/all_to_all | solution.py:21
  39.6 0.0 copy-start.2
  39.6 0.0 copy-start.4
  39.6 0.0 copy-start.5
  39.6 11.9 %all-to-all-start = ((bf16[1,32,3,128,256]{4,3,2,0,1:T(8,128)(2,1)}), bf16[1,32,3,128,256]{4,3,2,0,1:T(8,128)(2,1)}, u32[]{:S(2)}, u32[]{:S(2)}) async-start(bf16[1,32,3,128,256]{4,3,2,0,1:T(8,128)(2,1)} %bitcast.75), calls=%async_computation | async-start | bytes 12582912 | tf_op jit(solution)/shard_map/all_to_all | solution.py:30
  51.5 0.0 copy-start.3
  51.5 0.0 reduce-scatter.2.cloned.1.call-start
  51.6 0.0 copy-done.2
  51.6 0.1 fusion.19
  51.7 0.1 reduce_window_sum.11
  51.8 0.2 select_reduce_fusion
  52.0 0.0 copy-done.4
  52.0 0.0 copy-done.5
  52.0 0.2 fusion.22
  52.2 0.6 fusion.33
  52.7 0.7 iota_compare_fusion.2
  53.4 0.6 iota_compare_fusion.1
  54.0 2.3 convert_reduce_fusion
  56.3 2.1 fusion.1
  58.4 0.0 copy-done.3
  58.4 0.9 multiply_convert_fusion
  59.3 0.0 copy-start.1
  59.3 0.8 copy-done.1
  60.2 127.3 %all-to-all-done = bf16[1,32,3,128,256]{4,3,2,0,1:T(8,128)(2,1)} async-done(((bf16[1,32,3,128,256]{4,3,2,0,1:T(8,128)(2,1)}), bf16[1,32,3,128,256]{4,3,2,0,1:T(8,128)(2,1)}, u32[]{:S(2)}, u32[]{:S(2)}) %all-to-all-start) | async-done | bytes 6291488 | tf_op jit(solution)/shard_map/all_to_all | solution.py:30
  187.5 5.6 %gather_fusion = bf16[64,128,256]{2,1,0:T(8,128)(2,1)} fusion(bf16[96,128,256]{2,1,0:T(8,128)(2,1)} %bitcast.1, s32[1024]{0:T(1024)S(1)} %pad_clamp_fusion), kind=kCustom, calls=%fused_computation | custom fusion | bytes 8388864 | tf_op jit(solution)/shard_map/gather | solution.py:39
  193.1 15.1 %reshape.101 = bf16[2,4096,2,2,64]{4,3,2,1,0:T(2,128)(2,1)} reshape(bf16[64,128,256]{2,1,0:T(8,128)(2,1)} %gather_fusion) | data formatting | bytes 8388608 | tf_op jit(solution)/shard_map/reshape | solution.py:39
  208.1 19.4 %fusion.32 = (bf16[1,4096,2,1,64]{4,3,2,1,0:T(2,128)(2,1)}, bf16[1,4096,2,1,64]{4,3,2,1,0:T(2,128)(2,1)}, bf16[1,4096,2,1,64]{4,3,2,1,0:T(2,128)(2,1)}, bf16[1,4096,2,1,64]{4,3,2,1,0:T(2,128)(2,1)}) fusion(bf16[2,4096,2,2,64]{4,3,2,1,0:T(2,128)(2,1)} %reshape.101), kind=kLoop, calls=%fused_computation.53 | loop fusion | bytes 8388608 | tf_op jit(solution)/shard_map/slice | solution.py:48
  227.5 9.4 %copy.45 = bf16[1,4096,2,1,64]{1,4,2,3,0:T(8,128)(2,1)} copy(bf16[1,4096,2,1,64]{4,3,2,1,0:T(2,128)(2,1)} %get-tuple-element.11) | data formatting | bytes 2097152
  237.0 9.5 %copy.47 = bf16[1,4096,2,1,64]{1,4,2,3,0:T(8,128)(2,1)} copy(bf16[1,4096,2,1,64]{4,3,2,1,0:T(2,128)(2,1)} %get-tuple-element.13) | data formatting | bytes 2097152
  246.4 8.4 %copy.48 = bf16[1,4096,2,1,64]{1,4,2,3,0:T(8,128)(2,1)S(1)} copy(bf16[1,4096,2,1,64]{4,3,2,1,0:T(2,128)(2,1)} %get-tuple-element.12) | data formatting | bytes 2097152
  254.8 9.4 %copy.50 = bf16[1,4096,2,1,64]{1,4,2,3,0:T(8,128)(2,1)} copy(bf16[1,4096,2,1,64]{4,3,2,1,0:T(2,128)(2,1)} %get-tuple-element.14) | data formatting | bytes 2097152
  264.2 9.0 %fusion.5 = bf16[1,512,2,64]{1,3,2,0:T(8,128)(2,1)S(1)} fusion(pred[4096]{0:T(1024)(128)(4,1)S(1)} %iota_compare_fusion.2, bf16[1,4096,2,1,64]{1,4,2,3,0:T(8,128)(2,1)} %copy.47, bf16[1,4096,2,1,64]{1,4,2,3,0:T(8,128)(2,1)} %copy.45, bf16[1024,2,2,64]{0,3,2,1:T(8,128)(2,1)} %bitcast.80), kind=kOutput, calls=%fused_computation.11 | convolution fusion | flops 1103101952 | bytes 2363392 | tf_op jit(solution)/shard_map/hcp,phd->chd/dot_general | solution.py:56
  273.2 9.3 %fusion.4 = bf16[1,512,2,64]{1,3,2,0:T(8,128)(2,1)} fusion(pred[4096]{0:T(1024)(128)(4,1)S(1)} %iota_compare_fusion.1, bf16[1,4096,2,1,64]{1,4,2,3,0:T(8,128)(2,1)} %copy.50, bf16[1,4096,2,1,64]{1,4,2,3,0:T(8,128)(2,1)S(1)} %copy.48, bf16[1024,2,2,64]{0,3,2,1:T(8,128)(2,1)} %bitcast.81), kind=kOutput, calls=%fused_computation.10 | convolution fusion | flops 1103101952 | bytes 2363392 | tf_op jit(solution)/shard_map/hcp,phd->chd/dot_general | solution.py:56
  282.5 1.0 fusion.31
  283.5 0.9 fusion.15
  284.5 0.4 copy.42
  284.9 0.1 copy.51
  285.0 12.7 %all-reduce = (f32[1024]{0:T(1024)S(1)}, f32[1024]{0:T(1024)S(1)}) all-reduce(f32[1024]{0:T(1024)S(1)} %bitcast.85, f32[1024]{0:T(1024)S(1)} %bitcast.84), channel_id=1, replica_groups=mesh['req'=32,'head'=8] {'head'}, use_global_device_ids=true, to_apply=%region_8.9 | all-reduce | flops 2048 | bytes 16384 | tf_op jit(solution)/shard_map/psum | solution.py:61
  297.7 0.0 copy-done
  297.7 2.7 fusion.13
  300.4 0.0 reduce-scatter.2.cloned.1.call-update
  300.4 42.4 %reduce-scatter.2.cloned.1.call-done = f32[128,1024]{1,0:T(8,128)} async-done(((f32[1024,1024]{1,0:T(8,128)}), f32[128,1024]{1,0:T(8,128)}) %reduce-scatter.2.cloned.1.call-update) | async-done | bytes 524304 | tf_op jit(solution)/shard_map/reduce_scatter | solution.py:72
  342.8 1.8 convert_element_type.69
  (8 shorter events, 0.1 us)
Async XLA Ops:
  6.5 291.2 %copy-start = (bf16[1024,1024]{1,0:T(8,128)(2,1)S(1)}, bf16[1024,1024]{1,0:T(8,128)(2,1)}, u32[]{:S(2)}) copy-start(bf16[1024,1024]{1,0:T(8,128)(2,1)} %param.9) | copy-start | bytes 6291460
  39.6 12.0 %copy-start.2 = (s32[64,1]{0,1:T(1,128)S(1)}, s32[64,1]{0,1:T(1,128)}, u32[]{:S(2)}) copy-start(s32[64,1]{0,1:T(1,128)} %param.13) | copy-start | bytes 772
  39.6 12.4 %copy-start.4 = (s32[64]{0:T(128)S(1)}, s32[64]{0:T(128)}, u32[]{:S(2)}) copy-start(s32[64]{0:T(128)} %param.12) | copy-start | bytes 772
  39.6 12.4 %copy-start.5 = (s32[2]{0:T(128)S(1)}, s32[2]{0:T(128)}, u32[]{:S(2)}) copy-start(s32[2]{0:T(128)} %param.11) | copy-start | bytes 28
  39.6 147.9 %all-to-all-start = ((bf16[1,32,3,128,256]{4,3,2,0,1:T(8,128)(2,1)}), bf16[1,32,3,128,256]{4,3,2,0,1:T(8,128)(2,1)}, u32[]{:S(2)}, u32[]{:S(2)}) async-start(bf16[1,32,3,128,256]{4,3,2,0,1:T(8,128)(2,1)} %bitcast.75), calls=%async_computation | async-start | bytes 12582912 | tf_op jit(solution)/shard_map/all_to_all | solution.py:30
  51.5 6.9 %copy-start.3 = (bf16[1024,256]{1,0:T(8,128)(2,1)S(1)}, bf16[1024,256]{1,0:T(8,128)(2,1)}, u32[]{:S(2)}) copy-start(bf16[1024,256]{1,0:T(8,128)(2,1)} %param.8) | copy-start | bytes 1572868
  51.5 291.2 %reduce-scatter.2.cloned.1.call-start = ((), (), s32[]{:S(2)}) async-start(), calls=%async_computation.3 | async-start | bytes 4718592 | tf_op jit(solution)/shard_map/reduce_scatter | solution.py:72
  59.3 0.8 copy-start.1
Sparse Core Ops, SparseCore 0:
  300.5 42.1 reduce-scatter.1
